TPU v7x, 512 devices: a whole 4x8x8 slice. The times are simulated.
512 devices in a mesh: worker: 16 (over x, z_lo, core), fsdp: 32 (over z_hi, y).
Axes of the slice: x: 4, y: 8, z: 8 (z_hi: 4, z_lo: 2; z = z_hi * 2 + z_lo), core: 2. Of those that a mesh axis runs over, the one named last changes fastest.
Arguments:
- hidden: bfloat16 [9472, 65536], P('fsdp', 'worker'), may hold values from -6 to 6
- cotangent: bfloat16 [65536, 1792], P(('worker', 'fsdp')), may hold values from -6 to 6
- first_moment: bfloat16 [16, 9472, 1792], P('worker', 'fsdp'), may hold values from -0.0625 to 0.0625
- second_moment: bfloat16 [16, 9472, 1792], P('worker', 'fsdp'), may hold values from 1.21593475e-05 to 0.00024414062
- outer_momentum: bfloat16 [9472, 1792], P('fsdp', 'worker'), may hold values from -4 to 4
Outputs:
- new_momentum: float32 [9472, 1792], P('fsdp', 'worker')
All inputs are finite; a program needn't handle non-finite values.
Results may differ from a plain program's by a relative error of at most 0.0003.
Values may be sent and summed in bfloat16 or wider, within the bound.
No kernel may reach another device: no remote copies, remote signals or barrier semaphores. Data moves between devices by JAX's collectives and lax.ppermute only.
A program may use at most 64 MiB of HBM per device.

v0:
```python
import jax
import jax.numpy as jnp
from jax import lax
from jax.sharding import Mesh
from jax.sharding import PartitionSpec as P

W = ("wx", "wz", "wc")
F = ("fz", "fy")
SPLIT = {"worker": (4, 2, 2), "fsdp": (4, 8)}


def shards(hidden, cotangent, first_moment, second_moment, outer_momentum):
    gathered = lax.all_gather(cotangent, ("fy", "fz"), axis=0, tiled=True)
    nz, ny = SPLIT["fsdp"]
    rows, tokens = hidden.shape
    reordered = (
        hidden.reshape(rows, nz, ny, tokens // (nz * ny))
        .transpose(0, 2, 1, 3)
        .reshape(rows, tokens)
    )
    gradient = jnp.dot(reordered, gathered, preferred_element_type=jnp.float32) / gathered.shape[0]
    first_new = 0.9 * first_moment[0].astype(jnp.float32) + 0.1 * gradient
    second_new = 0.95 * second_moment[0].astype(jnp.float32) + 0.05 * gradient * gradient
    pseudo = first_new / (jnp.sqrt(second_new) + 1e-08)
    workers = lax.axis_size(W)
    cols = pseudo.shape[1]
    blocks = pseudo.reshape(rows, workers, cols // workers)
    received = lax.all_to_all(blocks, W, 1, 1, tiled=True)
    average = received.sum(axis=1) / workers
    return 0.9 * outer_momentum.astype(jnp.float32) + average


def solution(mesh):
    fine = Mesh(mesh.devices.reshape(SPLIT["worker"] + SPLIT["fsdp"]), W + F)
    in_specs = (P(F, W), P(W + F, None), P(W, F, None), P(W, F, None), P(F, W))
    out_specs = P(F, W)
    return jax.shard_map(shards, mesh=fine, in_specs=in_specs, out_specs=out_specs, check_vma=False)
```

profile of v0, /device:TPU:1, one launch (start us, length us, event | category | flops | bytes accessed | tf_op | source)
XLA Modules:
  0.0 275.4 jit_solution(3912588997436417546)
XLA Ops:
  6.5 0.0 all-gather.2.cloned.1.call-start
  6.5 0.7 all-gather.2.cloned.1.call-update
  7.3 2.2 copy.9
  9.5 1.2 copy.11
  10.7 0.0 copy-start.1
  10.7 3.2 %reshape.16 = bf16[296,4096]{1,0:T(8,128)(2,1)} reshape(bf16[296,8,4,128]{3,2,1,0:T(4,128)(2,1)S(1)} %bitcast.20) | data formatting | bytes 4849664 | tf_op jit(solution)/shard_map/reshape | solution.py:19
  14.0 177.4 %all-gather.2.cloned.1.call-done = bf16[4096,1792]{1,0:T(8,128)(2,1)} async-done(((bf16[128,1792]{1,0:T(8,128)(2,1)}), bf16[4096,1792]{1,0:T(8,128)(2,1)}) %all-gather.2.cloned.1.call-update) | async-done | bytes 14680080 | tf_op jit(solution)/shard_map/all_gather | solution.py:13
  191.3 0.0 copy-done.1
  191.3 12.9 %fusion.2 = f32[296,1792]{1,0:T(8,128)} fusion(bf16[1,296,1792]{2,1,0:T(8,128)(2,1)S(1)} %copy-done.1, bf16[1,296,1792]{2,1,0:T(8,128)(2,1)} %param.7, bf16[296,4096]{1,0:T(8,128)(2,1)} %reshape.16, bf16[4096,1792]{1,0:T(8,128)(2,1)} %all-gather.2.cloned.1.call-done), kind=kOutput, calls=%fused_computation.4 | convolution fusion | flops 4351664128 | bytes 21348352 | tf_op jit(solution)/shard_map/dot_general | solution.py:21
  204.2 3.0 %reshape.17 = f32[296,16,112]{2,1,0:T(8,128)S(1)} reshape(f32[296,1792]{1,0:T(8,128)} %fusion.2) | data formatting | bytes 4243456 | tf_op jit(solution)/shard_map/reshape | solution.py:27
  207.2 0.8 copy.8
  208.0 59.0 %all_to_all.5 = f32[296,16,112]{2,0,1:T(8,128)S(1)} all-to-all(f32[296,16,112]{2,0,1:T(8,128)S(1)} %copy.8), channel_id=1, replica_groups=mesh['wx'=4,'wz'=2,'wc'=2,'fz'=4,'fy'=8] {'wx','wz','wc'}, dimensions={1} | all-to-all | bytes 4243456 | tf_op jit(solution)/shard_map/all_to_all | solution.py:28
  267.0 0.0 copy-start
  267.0 0.2 reduce_sum.9
  267.2 0.7 copy-done
  267.9 0.7 multiply_add_fusion
Async XLA Ops:
  6.5 184.8 %all-gather.2.cloned.1.call-start = ((), (), s32[]{:S(2)}) async-start(), calls=%async_computation.1 | async-start | bytes 15138816 | tf_op jit(solution)/shard_map/all_gather | solution.py:13
  10.7 180.6 %copy-start.1 = (bf16[1,296,1792]{2,1,0:T(8,128)(2,1)S(1)}, bf16[1,296,1792]{2,1,0:T(8,128)(2,1)}, u32[]{:S(2)}) copy-start(bf16[1,296,1792]{2,1,0:T(8,128)(2,1)} %param.8) | copy-start | bytes 3182596
  267.0 0.9 copy-start
Sparse Core Ops, SparseCore 0:
  10.5 180.7 all-gather.1
where the time goes:
time: 276 us; the launch traced here: 275 us
  waiting for transfers between devices  178 us (64%)
  blocking collectives  59 us (21%)
  between operations  13.4 us (5%)
  matrix products  12.9 us (5%)
  local copies, waits for them, and re-layouts  11.2 us (4%)
    all_gather x1, waiting for transfers between devices, shards(): gathered = lax.all_gather(cotangent, ('fy', 'fz'), axis=0, tiled=True)  177 us
    all_to_all x1, blocking collectives, shards(): received = lax.all_to_all(blocks, W, 1, 1, tiled=True)  59 us
    dot_general x1, matrix products, shards(): jnp.dot(reordered, gathered, preferred_element_type=jnp.float32)  12.9 us
  transfers between devices with their start and end apart: 1, of which 1 were waited for; matrix products, arithmetic and copies ran while one was open for 2% of the time, Pallas kernels for 0%

commit v1 on v0

--- a/solution.py
+++ b/solution.py
@@ -25,7 +25,9 @@
     workers = lax.axis_size(W)
     cols = pseudo.shape[1]
     blocks = pseudo.reshape(rows, workers, cols // workers)
-    received = lax.all_to_all(blocks, W, 1, 1, tiled=True)
+    received = jnp.concatenate(
+        lax.all_to_all(jnp.stack(jnp.split(blocks, lax.axis_size(W), axis=1)), W, 0, 0), axis=1
+    )
     average = received.sum(axis=1) / workers
     return 0.9 * outer_momentum.astype(jnp.float32) + average
 

time: 276 us -> 277 us (level)
  no operation moved by 1% of the time
where the time goes in v1:
time: 277 us
  waiting for transfers between devices  178 us (64%)
  blocking collectives  59 us (21%)
  between operations  13.6 us (5%)
  matrix products  12.9 us (5%)
  local copies, waits for them, and re-layouts  12.3 us (4%)
    all_gather x1, waiting for transfers between devices, shards(): gathered = lax.all_gather(cotangent, ('fy', 'fz'), axis=0, tiled=True)  177 us
    all_to_all x1, blocking collectives, shards(): lax.all_to_all(jnp.stack(jnp.split(blocks, lax.axis_size(W), axis=1)), W,...  59 us
    dot_general x1, matrix products, shards(): jnp.dot(reordered, gathered, preferred_element_type=jnp.float32)  12.9 us
  transfers between devices with their start and end apart: 1, of which 1 were waited for; matrix products, arithmetic and copies ran while one was open for 2% of the time, Pallas kernels for 0%

profile of v1, /device:TPU:1, one launch (start us, length us, event | category | flops | bytes accessed | tf_op | source)
XLA Modules:
  0.0 276.7 jit_solution(4616423825716961269)
XLA Ops:
  6.5 0.0 all-gather.2.cloned.1.call-start
  6.5 0.7 all-gather.2.cloned.1.call-update
  7.3 2.2 copy.52
  9.5 1.2 copy.54
  10.7 0.0 copy-start.1
  10.7 3.2 %reshape.18 = bf16[296,4096]{1,0:T(8,128)(2,1)} reshape(bf16[296,8,4,128]{3,2,1,0:T(4,128)(2,1)S(1)} %bitcast.66) | data formatting | bytes 4849664 | tf_op jit(solution)/shard_map/reshape | solution.py:19
  14.0 177.3 %all-gather.2.cloned.1.call-done = bf16[4096,1792]{1,0:T(8,128)(2,1)} async-done(((bf16[128,1792]{1,0:T(8,128)(2,1)}), bf16[4096,1792]{1,0:T(8,128)(2,1)}) %all-gather.2.cloned.1.call-update) | async-done | bytes 14680080 | tf_op jit(solution)/shard_map/all_gather | solution.py:13
  191.3 0.0 copy-done.1
  191.3 12.9 %fusion.2 = f32[296,1792]{1,0:T(8,128)} fusion(bf16[1,296,1792]{2,1,0:T(8,128)(2,1)S(1)} %copy-done.1, bf16[1,296,1792]{2,1,0:T(8,128)(2,1)} %param.7, bf16[296,4096]{1,0:T(8,128)(2,1)} %reshape.18, bf16[4096,1792]{1,0:T(8,128)(2,1)} %all-gather.2.cloned.1.call-done), kind=kOutput, calls=%fused_computation.4 | convolution fusion | flops 4351664128 | bytes 21348352 | tf_op jit(solution)/shard_map/dot_general | solution.py:21
  204.2 3.0 %reshape.19 = f32[296,16,112]{2,1,0:T(8,128)S(1)} reshape(f32[296,1792]{1,0:T(8,128)} %fusion.2) | data formatting | bytes 4243456 | tf_op jit(solution)/shard_map/reshape | solution.py:27
  207.2 1.7 fusion.3
  209.3 59.0 %all_to_all.5 = f32[16,296,1,112]{3,1,2,0:T(8,128)S(1)} all-to-all(f32[16,296,1,112]{3,1,2,0:T(8,128)S(1)} %constant_dynamic-update-slice_fusion), channel_id=1, replica_groups=mesh['wx'=4,'wz'=2,'wc'=2,'fz'=4,'fy'=8] {'wx','wz','wc'}, dimensions={0} | all-to-all | bytes 4243456 | tf_op jit(solution)/shard_map/all_to_all | solution.py:29
  268.3 0.0 copy-start
  268.3 0.2 reduce_sum.9
  268.4 0.7 copy-done
  269.1 0.7 multiply_add_fusion
  (16 shorter events, 0.2 us)
Async XLA Ops:
  6.5 184.8 %all-gather.2.cloned.1.call-start = ((), (), s32[]{:S(2)}) async-start(), calls=%async_computation.1 | async-start | bytes 15138816 | tf_op jit(solution)/shard_map/all_gather | solution.py:13
  10.7 180.6 %copy-start.1 = (bf16[1,296,1792]{2,1,0:T(8,128)(2,1)S(1)}, bf16[1,296,1792]{2,1,0:T(8,128)(2,1)}, u32[]{:S(2)}) copy-start(bf16[1,296,1792]{2,1,0:T(8,128)(2,1)} %param.8) | copy-start | bytes 3182596
  268.3 0.9 copy-start
Sparse Core Ops, SparseCore 0:
  10.5 180.7 all-gather.1
